TPU v7x, 128 devices: a whole 4x4x4 slice. The times are simulated.
128 devices in a mesh: dp: 4 (over z), rows: 32 (over y, x, core).
Axes of the slice: x: 4, y: 4, z: 4, core: 2. Of those that a mesh axis runs over, the one named last changes fastest.
Arguments:
- images: bfloat16 [4, 64, 256, 2048], P('dp', None, 'rows'), may hold values from -1000 to 1000
- conv_w: float32 [576, 64], replicated, may hold values from -0.25 to 0.25
- bias: float32 [64], replicated, may hold values from -4 to 4
- cotangent: bfloat16 [4, 64, 256, 2048], P('dp', None, 'rows'), may hold values from -1500 to 1500
Outputs:
- outputs: bfloat16 [4, 64, 256, 2048], P('dp', None, 'rows')
- grad_x: bfloat16 [4, 64, 256, 2048], P('dp', None, 'rows')
- grad_w: float32 [576, 64], replicated
All inputs are finite; a program needn't handle non-finite values.
Results may differ from a plain program's by a relative error of at most 0.0017.
The roundings to bfloat16 on the way count: a program that leaves them out, or rounds other values in their place, can miss the bound.
Values may be sent and summed in bfloat16 or wider, within the bound.
No kernel may reach another device: no remote copies, remote signals or barrier semaphores. Data moves between devices by JAX's collectives and lax.ppermute only.
A program may use at most 128 MiB of HBM per device.

v0:
```python
import jax
import jax.numpy as jnp
from jax import lax
from jax.sharding import PartitionSpec as P

ITERS = 5


eps_value = 1e-05


def with_halo(block, sides, width):
    for axis, dim in sides:
        count = lax.axis_size(axis)
        forward = [(i, i + 1) for i in range(count - 1)]
        backward = [(target, source) for source, target in forward]
        low = lax.ppermute(
            lax.slice_in_dim(block, block.shape[dim] - width, None, axis=dim), axis, forward
        )
        high = lax.ppermute(lax.slice_in_dim(block, 0, width, axis=dim), axis, backward)
        block = jnp.concatenate([low, block, high], axis=dim)
    return block


def tap_stack(padded, strip_rows, img_width, flipped):
    shifted = [padded[:, :, first_col : first_col + img_width] for first_col in range(3)]
    pieces = []
    for tap_row in range(3):
        for tap_col in range(3):
            first_row = 2 - tap_row if flipped else tap_row
            first_col = 2 - tap_col if flipped else tap_col
            pieces.append(shifted[first_col][first_row : first_row + strip_rows])
    return pieces


def tree_psum(block, axes, levels):
    size = 1
    for axis in axes:
        size *= lax.axis_size(axis)
    index = 0
    for axis in axes:
        index = index * lax.axis_size(axis) + lax.axis_index(axis)
    trail = []
    for stride, radix in levels:
        digit = (index // stride) % radix
        parts = block.reshape((radix, block.shape[0] // radix) + block.shape[1:])
        block = lax.dynamic_index_in_dim(parts, digit, 0, keepdims=False)
        shifts = []
        for shift in range(1, radix):
            pairs = [
                (i, i + ((((i // stride) % radix) + shift) % radix - (i // stride) % radix) * stride)
                for i in range(size)
            ]
            send = lax.dynamic_index_in_dim(parts, (digit + shift) % radix, 0, keepdims=False)
            block = block + lax.ppermute(send, axes, pairs)
            shifts.append(pairs)
        trail.append((radix, digit, shifts))
    for radix, digit, shifts in reversed(trail):
        pieces = [block] + [lax.ppermute(block, axes, pairs) for pairs in shifts]
        placed = []
        for position in range(radix):
            source = (digit - position) % radix
            value = pieces[0]
            for shift in range(1, radix):
                value = jnp.where(source == shift, pieces[shift], value)
            placed.append(value)
        block = jnp.concatenate(placed, axis=0)
    return block


def physical_levels(mesh_sizes):
    levels, stride, rest = [], 1, mesh_sizes
    if rest % 2 == 0 and rest > 2 and ((rest // 2) & (rest // 2 - 1)) == 0 and (rest // 2).bit_length() % 2 == 1:
        levels.append((1, 2))
        stride, rest = 2, rest // 2
    while rest % 4 == 0:
        levels.append((stride, 4))
        stride, rest = stride * 4, rest // 4
    while rest % 2 == 0:
        levels.append((stride, 2))
        stride, rest = stride * 2, rest // 2
    return levels


def on_device(images, conv_w, bias, cotangent):
    highest = lax.Precision.HIGHEST
    channels = images.shape[1]
    strip_rows = images.shape[2]
    img_width = images.shape[3]
    patch_dim = 9 * channels
    pixels = images.shape[0] * strip_rows * img_width * lax.axis_size("rows") * lax.axis_size("dp")
    rows_first = images[0].transpose(1, 0, 2)
    grad_first = cotangent[0].transpose(1, 0, 2)
    framed = with_halo(rows_first, (("rows", 0),), 1)
    gframed = with_halo(grad_first, (("rows", 0),), 1)
    padded = jnp.pad(framed, ((0, 0), (0, 0), (1, 1)))
    gpadded = jnp.pad(gframed, ((0, 0), (0, 0), (1, 1)))
    contract_pixels = (((0, 2), (0, 2)), ((), ()))

    stacked = jnp.concatenate(tap_stack(padded, strip_rows, img_width, False) + [grad_first], axis=1)
    moments = lax.dot_general(
        stacked, stacked, contract_pixels, preferred_element_type=jnp.float32
    )
    sums = jnp.sum(stacked, axis=(0, 2), dtype=jnp.float32)
    local = jnp.concatenate([moments, sums[:, None]], axis=1)
    world = lax.axis_size("dp") * lax.axis_size("rows")
    total = tree_psum(local, ("dp", "rows"), physical_levels(world))

    gram_whole = total[:patch_dim, :patch_dim]
    cross_total = total[:patch_dim, patch_dim : patch_dim + channels]
    patch_sums = total[:patch_dim, -1]
    grad_sum = total[patch_dim:, -1]

    mean_vec = patch_sums / pixels
    identity = jnp.eye(patch_dim, dtype=jnp.float32)
    covariance = gram_whole / pixels - jnp.outer(mean_vec, mean_vec) + eps_value * identity
    frob_norm = jnp.sqrt(jnp.sum(covariance * covariance))
    iter_y = covariance / frob_norm
    factor = 0.5 * (3.0 * identity - iter_y)
    iter_y = jnp.dot(factor, iter_y, precision=highest)
    iter_z = factor
    for sweep in range(1, ITERS):
        factor = 0.5 * (3.0 * identity - jnp.dot(iter_z, iter_y, precision=highest))
        if sweep < ITERS - 1:
            iter_y = jnp.dot(factor, iter_y, precision=highest)
        iter_z = jnp.dot(factor, iter_z, precision=highest)
    inv_root = iter_z / jnp.sqrt(frob_norm)
    mixing = jnp.dot(inv_root, conv_w, precision=highest)
    mixing_b = mixing.astype(jnp.bfloat16)
    bias_shift = bias - jnp.dot(mean_vec, mixing, precision=highest)
    grad_w = (
        jnp.dot(inv_root.T, cross_total - jnp.outer(mean_vec, grad_sum), precision=highest)
        / pixels
    )
    back_w = mixing_b.reshape(9, channels, channels).transpose(1, 0, 2).reshape(channels, patch_dim)
    contract_taps = (((0,), (1,)), ((), ()))
    out_rows = lax.dot_general(
        mixing_b, stacked[:, :patch_dim], contract_taps, preferred_element_type=jnp.float32
    )
    out_buffer = (out_rows + bias_shift[:, None, None]).astype(jnp.bfloat16)
    gstacked = jnp.concatenate(tap_stack(gpadded, strip_rows, img_width, True), axis=1)
    contract_back = (((1,), (1,)), ((), ()))
    back_rows = lax.dot_general(
        back_w, gstacked, contract_back, preferred_element_type=jnp.float32
    )
    back_buffer = back_rows.astype(jnp.bfloat16)
    return (out_buffer[None], back_buffer[None], grad_w)


def solution(mesh):
    placed = (P("dp", None, "rows", None), P(), P(), P("dp", None, "rows", None))
    return jax.shard_map(
        on_device,
        mesh=mesh,
        in_specs=placed,
        out_specs=(P("dp", None, "rows", None), P("dp", None, "rows", None), P()),
        check_vma=False,
    )
```

profile of v0, /device:TPU:1, one launch (start us, length us, event | category | flops | bytes accessed | tf_op | source)
XLA Modules:
  0.0 263.1 jit_solution(5229823577989239971)
XLA Ops:
  0.7 2.9 %copy.32 = bf16[1,64,8,2048]{3,1,2,0:T(8,128)(2,1)S(1)} copy(bf16[1,64,8,2048]{3,2,1,0:T(8,128)(2,1)} %param.7) | data formatting | bytes 4194304 | tf_op args[3]
  4.5 3.3 %collective-permute-start.23 = (bf16[1,64,2048]{2,1,0:T(8,128)(2,1)}, bf16[1,64,2048]{2,1,0:T(8,128)(2,1)S(1)}, u32[]{:S(2)}, u32[]{:S(2)}) collective-permute-start(bf16[1,64,2048]{2,1,0:T(8,128)(2,1)} %get-tuple-element.16), channel_id=1, source_target_pairs={{1,0},{2,1},{3,2},{4,3},{5,4},{6,5},{7,6},{8,7},{9,8},{10,9},{11,1... | collective-permute-start | bytes 786440 | tf_op jit(solution)/shard_map/ppermute | solution.py:20
  7.7 3.1 %collective-permute-start.22 = (bf16[1,64,2048]{2,1,0:T(8,128)(2,1)}, bf16[1,64,2048]{2,1,0:T(8,128)(2,1)S(1)}, u32[]{:S(2)}, u32[]{:S(2)}) collective-permute-start(bf16[1,64,2048]{2,1,0:T(8,128)(2,1)} %get-tuple-element.15), channel_id=1, source_target_pairs={{0,1},{1,2},{2,3},{3,4},{4,5},{5,6},{6,7},{7,8},{8,9},{9,10},{10,1... | collective-permute-start | bytes 786440 | tf_op jit(solution)/shard_map/ppermute | solution.py:17
  16.1 3.8 %collective-permute-start = (bf16[1,64,2048]{2,1,0:T(8,128)(2,1)}, bf16[1,64,2048]{2,1,0:T(8,128)(2,1)S(1)}, u32[]{:S(2)}, u32[]{:S(2)}) collective-permute-start(bf16[1,64,2048]{2,1,0:T(8,128)(2,1)} %get-tuple-element.17), channel_id=1, source_target_pairs={{0,1},{1,2},{2,3},{3,4},{4,5},{5,6},{6,7},{7,8},{8,9},{9,10},{10,1... | collective-permute-start | bytes 786440 | tf_op jit(solution)/shard_map/ppermute | solution.py:17
  27.7 2.8 %slice_dynamic-update-slice_fusion.3 = bf16[8,576,2048]{2,1,0:T(8,128)(2,1)} fusion(bf16[8,576,2048]{2,1,0:T(8,128)(2,1)} %slice_dynamic-update-slice_fusion.4, bf16[10,64,2050]{2,1,0:T(8,128)(2,1)S(1)} %select_maximum_fusion), kind=kLoop, calls=%fused_computation.29 | loop fusion | bytes 4194304
  48.9 3.1 %slice_dynamic-update-slice_fusion.7 = (bf16[8,640,2048]{2,1,0:T(8,128)(2,1)}, bf16[8,576,2048]{2,1,0:T(8,128)(2,1)}) fusion(bf16[8,640,2048]{2,1,0:T(8,128)(2,1)} %fusion.27, bf16[10,64,2050]{2,1,0:T(8,128)(2,1)S(1)} %select_maximum_fusion.2), kind=kLoop, calls=%fused_computation.41 | loop fusion | bytes 8388608
  52.1 4.1 %constant_dynamic-update-slice_fusion.3 = (bf16[8,576,2048]{2,1,0:T(8,128)(2,1)}, bf16[8,640,2048]{2,1,0:T(8,128)(2,1)}, bf16[8,576,2048]{2,1,0:T(8,128)(2,1)}) fusion(bf16[8,576,2048]{2,1,0:T(8,128)(2,1)} %slice_dynamic-update-slice_fusion.3, bf16[1,64,8,2048]{3,2,1,0:T(8,128)(2,1)S(1)} %copy-done.10, bf16[8,640,2048]{2,1,0:T(8,128)(2,1)} %get-tuple-element.11, ...), kind=kLoop, calls=%fused_computation.131 | loop fusion | flops 4194304 | bytes 10747904
  56.2 22.7 %fusion.83 = f32[640,640,1]{1,0,2:T(8,128)} fusion(bf16[8,640,2048]{2,1,0:T(8,128)(2,1)} %get-tuple-element.14), kind=kOutput, calls=%fused_computation.159 | convolution fusion | flops 13421772800 | bytes 22609920 | tf_op jit(solution)/shard_map/dot_general | solution.py:101
  78.9 8.6 %convert_reduce_fusion = f32[640]{0:T(1024)S(1)} fusion(bf16[8,640,2048]{2,1,0:T(8,128)(2,1)} %get-tuple-element.14), kind=kLoop, calls=%fused_computation | loop fusion | flops 20970880 | bytes 20974080 | tf_op jit(solution)/shard_map/reduce_sum | solution.py:104
  87.5 2.8 %slice_dynamic-update-slice_fusion.14 = bf16[8,576,2048]{2,1,0:T(8,128)(2,1)} fusion(bf16[8,576,2048]{2,1,0:T(8,128)(2,1)} %get-tuple-element.44, bf16[10,64,2050]{2,1,0:T(8,128)(2,1)S(1)} %select_maximum_fusion.2), kind=kLoop, calls=%fused_computation.48 | loop fusion | bytes 4194304
  96.7 6.7 %collective-permute-start.5 = (f32[80,641]{1,0:T(8,128)S(1)}, f32[80,641]{1,0:T(8,128)S(1)}, u32[]{:S(2)}, u32[]{:S(2)}) collective-permute-start(f32[80,641]{1,0:T(8,128)S(1)} %get-tuple-element.26), channel_id=1, source_target_pairs={{0,6},{1,7},{2,0},{3,1},{4,2},{5,3},{6,4},{7,5},{8,14},{9,15},{10,... | collective-permute-start | bytes 615368 | tf_op jit(solution)/shard_map/ppermute | solution.py:55
  106.9 7.1 %collective-permute-done.5 = f32[80,641]{1,0:T(8,128)S(1)} collective-permute-done((f32[80,641]{1,0:T(8,128)S(1)}, f32[80,641]{1,0:T(8,128)S(1)}, u32[]{:S(2)}, u32[]{:S(2)}) %collective-permute-start.5) | collective-permute-done | bytes 205152 | tf_op jit(solution)/shard_map/ppermute | solution.py:55
  114.0 3.5 %collective-permute-done.3 = f32[80,641]{1,0:T(8,128)S(1)} collective-permute-done((f32[80,641]{1,0:T(8,128)S(1)}, f32[80,641]{1,0:T(8,128)S(1)}, u32[]{:S(2)}, u32[]{:S(2)}) %collective-permute-start.3) | collective-permute-done | bytes 205152 | tf_op jit(solution)/shard_map/ppermute | solution.py:55
  119.4 3.1 %collective-permute-start.7 = (f32[20,641]{1,0:T(8,128)S(1)}, f32[20,641]{1,0:T(8,128)S(1)}, u32[]{:S(2)}, u32[]{:S(2)}) collective-permute-start(f32[20,641]{1,0:T(8,128)S(1)} %get-tuple-element.34), channel_id=1, source_target_pairs={{0,16},{1,17},{2,18},{3,19},{4,20},{5,21},{6,22},{7,23},{8,24},{9,... | collective-permute-start | bytes 153848 | tf_op jit(solution)/shard_map/ppermute | solution.py:55
  128.4 3.8 %collective-permute-start.11 = (f32[5,641]{1,0:T(8,128)S(1)}, f32[5,641]{1,0:T(8,128)S(1)}, u32[]{:S(2)}, u32[]{:S(2)}) collective-permute-start(f32[5,641]{1,0:T(8,128)S(1)} %get-tuple-element.40), channel_id=1, source_target_pairs={{0,96},{1,97},{2,98},{3,99},{4,100},{5,101},{6,102},{7,103},{8,104... | collective-permute-start | bytes 38468 | tf_op jit(solution)/shard_map/ppermute | solution.py:55
  133.0 3.1 %fusion.28 = bf16[8,576,2048]{2,1,0:T(8,128)(2,1)} fusion(bf16[8,576,2048]{2,1,0:T(8,128)(2,1)} %slice_dynamic-update-slice_fusion.8, bf16[1,64,2048]{2,1,0:T(8,128)(2,1)S(1)} %collective-permute-done.1, bf16[8,64,2048]{2,1,0:T(8,128)(2,1)} %bitcast.111), kind=kLoop, calls=%fused_computation.70 | loop fusion | flops 4194304 | bytes 4456448
  139.9 2.8 %slice_dynamic-update-slice_fusion.6 = bf16[8,576,2048]{2,1,0:T(8,128)(2,1)} fusion(bf16[8,576,2048]{2,1,0:T(8,128)(2,1)} %fusion.28, bf16[10,64,2050]{2,1,0:T(8,128)(2,1)S(1)} %select_maximum_fusion.2), kind=kLoop, calls=%fused_computation.40 | loop fusion | bytes 4194304 | tf_op jit(solution)/shard_map/concatenate | solution.py:100
  159.8 8.5 %collective-permute-start.21 = (f32[320,641]{1,0:T(8,128)S(1)}, f32[320,641]{1,0:T(8,128)S(1)}, u32[]{:S(2)}, u32[]{:S(2)}) collective-permute-start(f32[320,641]{1,0:T(8,128)S(1)} %pad_maximum_fusion.4), channel_id=1, source_target_pairs={{0,1},{1,0},{2,3},{3,2},{4,5},{5,4},{6,7},{7,6},{8,9},{9,8},{10,11... | collective-permute-start | bytes 2461448 | tf_op jit(solution)/shard_map/ppermute | solution.py:59
  174.4 6.4 %fusion.21 = f32[576,576]{1,0:T(8,128)S(1)} fusion(f32[576,576]{1,0:T(8,128)} %get-tuple-element.10, f32[]{:T(128)S(6)} %sqrt.6), kind=kOutput, calls=%fused_computation.66 | convolution fusion | flops 2295226368 | bytes 2654212 | tf_op jit(solution)/shard_map/dot_general | solution.py:120
  180.8 4.2 %fusion.11 = f32[576,576]{1,0:T(8,128)S(1)} fusion(f32[576,576]{1,0:T(8,128)S(1)} %fusion.21, f32[576,576]{1,0:T(8,128)S(1)} %copy-done.15, f32[]{:T(128)S(6)} %sqrt.6), kind=kOutput, calls=%fused_computation.57 | convolution fusion | flops 2296221696 | bytes 3981316 | tf_op jit(solution)/shard_map/dot_general | solution.py:123
  185.1 4.5 %fusion.17 = f32[576,576]{1,0:T(8,128)S(1)} fusion(f32[576,576]{1,0:T(8,128)S(1)} %fusion.11, f32[576,576]{1,0:T(8,128)S(1)} %copy-done.15, f32[]{:T(128)S(6)} %sqrt.6), kind=kOutput, calls=%fused_computation.64 | convolution fusion | flops 2294894592 | bytes 3981316 | tf_op jit(solution)/shard_map/dot_general | solution.py:126
  189.6 4.2 %fusion.84 = f32[576,576]{1,0:T(8,128)S(1)} fusion(f32[576,576]{1,0:T(8,128)S(1)} %fusion.11, f32[576,576]{1,0:T(8,128)S(1)} %fusion.21), kind=kOutput, calls=%fused_computation.160 | convolution fusion | flops 2293235712 | bytes 3981312 | tf_op jit(solution)/shard_map/dot_general | solution.py:125
  193.8 4.2 %fusion.12 = f32[576,576]{1,0:T(8,128)S(1)} fusion(f32[576,576]{1,0:T(8,128)S(1)} %fusion.17, f32[576,576]{1,0:T(8,128)S(1)} %fusion.84), kind=kOutput, calls=%fused_computation.58 | convolution fusion | flops 2294562816 | bytes 3981312 | tf_op jit(solution)/shard_map/dot_general | solution.py:123
  198.1 4.6 %fusion.85 = f32[576,576]{1,0:T(8,128)S(1)} fusion(f32[576,576]{1,0:T(8,128)S(1)} %fusion.12, f32[576,576]{1,0:T(8,128)S(1)} %fusion.17), kind=kOutput, calls=%fused_computation.161 | convolution fusion | flops 2293235712 | bytes 3981312 | tf_op jit(solution)/shard_map/dot_general | solution.py:126
  202.7 4.2 %fusion.86 = f32[576,576]{1,0:T(8,128)S(1)} fusion(f32[576,576]{1,0:T(8,128)S(1)} %fusion.12, f32[576,576]{1,0:T(8,128)S(1)} %fusion.84), kind=kOutput, calls=%fused_computation.162 | convolution fusion | flops 2293235712 | bytes 3981312 | tf_op jit(solution)/shard_map/dot_general | solution.py:125
  206.9 4.2 %fusion.13 = f32[576,576]{1,0:T(8,128)S(1)} fusion(f32[576,576]{1,0:T(8,128)S(1)} %fusion.85, f32[576,576]{1,0:T(8,128)S(1)} %fusion.86), kind=kOutput, calls=%fused_computation.59 | convolution fusion | flops 2294562816 | bytes 3981312 | tf_op jit(solution)/shard_map/dot_general | solution.py:123
  211.2 5.2 %fusion.87 = f32[576,576]{1,0:T(8,128)} fusion(f32[576,576]{1,0:T(8,128)S(1)} %fusion.13, f32[576,576]{1,0:T(8,128)S(1)} %fusion.85), kind=kOutput, calls=%fused_computation.163 | convolution fusion | flops 2293235712 | bytes 3981312 | tf_op jit(solution)/shard_map/dot_general | solution.py:126
  216.4 5.4 %fusion.88 = f32[576,576]{1,0:T(8,128)} fusion(f32[576,576]{1,0:T(8,128)S(1)} %fusion.13, f32[576,576]{1,0:T(8,128)S(1)} %fusion.86), kind=kOutput, calls=%fused_computation.164 | convolution fusion | flops 2293235712 | bytes 3981312 | tf_op jit(solution)/shard_map/dot_general | solution.py:125
  222.0 6.2 %fusion.89 = f32[576,576]{1,0:T(8,128)S(1)} fusion(f32[576,576]{1,0:T(8,128)} %fusion.87, f32[576,576]{1,0:T(8,128)} %fusion.88), kind=kOutput, calls=%fused_computation.165 | convolution fusion | flops 2293235712 | bytes 3981312 | tf_op jit(solution)/shard_map/dot_general | solution.py:123
  228.2 4.2 %fusion.29 = f32[576,576]{1,0:T(8,128)S(1)} fusion(f32[576,576]{1,0:T(8,128)S(1)} %copy-done.14, f32[576,576]{1,0:T(8,128)S(1)} %fusion.89, f32[]{:T(128)S(6)} %sqrt.7), kind=kOutput, calls=%fused_computation.71 | convolution fusion | flops 2294894592 | bytes 3981316 | tf_op jit(solution)/shard_map/dot_general | solution.py:126
  235.7 10.1 %fusion.3 = bf16[1,64,8,2048]{3,1,2,0:T(8,128)(2,1)S(1)} fusion(bf16[8,576,2048]{2,1,0:T(8,128)(2,1)} %slice_dynamic-update-slice_fusion.6, f32[64]{0:T(128)S(1)} %fusion.32, bf16[576,64]{0,1:T(8,128)(2,1)S(1)} %get-tuple-element.42), kind=kOutput, calls=%fused_computation.17 | convolution fusion | flops 1210056704 | bytes 21045504 | tf_op jit(solution)/shard_map/dot_general | solution.py:137
  248.4 10.0 %fusion.2 = bf16[1,64,8,2048]{3,1,2,0:T(8,128)(2,1)S(1)} fusion(bf16[64,576,1]{0,1,2:T(8,128)(2,1)S(1)} %bitcast.125, bf16[8,576,2048]{2,1,0:T(8,128)(2,1)} %slice_dynamic-update-slice_fusion), kind=kOutput, calls=%fused_computation.16 | convolution fusion | flops 1209008128 | bytes 21045248 | tf_op jit(solution)/shard_map/dot_general | solution.py:143
  (130 shorter events, 86.6 us)
Async XLA Ops:
  0.6 232.9 %copy-start = (f32[576,64]{0,1:T(8,128)S(1)}, f32[576,64]{0,1:T(8,128)}, u32[]{:S(2)}) copy-start(f32[576,64]{0,1:T(8,128)} %param.5) | copy-start | bytes 442372
  0.6 10.2 %copy-start.7 = (bf16[1,64,8,2048]{3,2,1,0:T(8,128)(2,1)S(1)}, bf16[1,64,8,2048]{3,2,1,0:T(8,128)(2,1)}, u32[]{:S(2)}) copy-start(bf16[1,64,8,2048]{3,2,1,0:T(8,128)(2,1)} %param.4) | copy-start | bytes 6291460
  3.6 21.1 %copy-start.5 = (bf16[1,64,8,2048]{3,1,2,0:T(8,128)(2,1)}, bf16[1,64,8,2048]{3,1,2,0:T(8,128)(2,1)S(1)}, u32[]{:S(2)}) copy-start(bf16[1,64,8,2048]{3,1,2,0:T(8,128)(2,1)S(1)} %copy.32) | copy-start | bytes 6291460
  4.5 16.1 %collective-permute-start.23 = (bf16[1,64,2048]{2,1,0:T(8,128)(2,1)}, bf16[1,64,2048]{2,1,0:T(8,128)(2,1)S(1)}, u32[]{:S(2)}, u32[]{:S(2)}) collective-permute-start(bf16[1,64,2048]{2,1,0:T(8,128)(2,1)} %get-tuple-element.16), channel_id=1, source_target_pairs={{1,0},{2,1},{3,2},{4,3},{5,4},{6,5},{7,6},{8,7},{9,8},{10,9},{11,1... | collective-permute-start | bytes 786440 | tf_op jit(solution)/shard_map/ppermute | solution.py:20
  7.7 12.8 %collective-permute-start.22 = (bf16[1,64,2048]{2,1,0:T(8,128)(2,1)}, bf16[1,64,2048]{2,1,0:T(8,128)(2,1)S(1)}, u32[]{:S(2)}, u32[]{:S(2)}) collective-permute-start(bf16[1,64,2048]{2,1,0:T(8,128)(2,1)} %get-tuple-element.15), channel_id=1, source_target_pairs={{0,1},{1,2},{2,3},{3,4},{4,5},{5,6},{6,7},{7,8},{8,9},{9,10},{10,1... | collective-permute-start | bytes 786440 | tf_op jit(solution)/shard_map/ppermute | solution.py:17
  14.2 16.2 %collective-permute-start.1 = (bf16[1,64,2048]{2,1,0:T(8,128)(2,1)}, bf16[1,64,2048]{2,1,0:T(8,128)(2,1)S(1)}, u32[]{:S(2)}, u32[]{:S(2)}) collective-permute-start(bf16[1,64,2048]{2,1,0:T(8,128)(2,1)} %get-tuple-element.18), channel_id=1, source_target_pairs={{1,0},{2,1},{3,2},{4,3},{5,4},{6,5},{7,6},{8,7},{9,8},{10,9},{11,1... | collective-permute-start | bytes 786440 | tf_op jit(solution)/shard_map/ppermute | solution.py:20
  16.1 14.3 %collective-permute-start = (bf16[1,64,2048]{2,1,0:T(8,128)(2,1)}, bf16[1,64,2048]{2,1,0:T(8,128)(2,1)S(1)}, u32[]{:S(2)}, u32[]{:S(2)}) collective-permute-start(bf16[1,64,2048]{2,1,0:T(8,128)(2,1)} %get-tuple-element.17), channel_id=1, source_target_pairs={{0,1},{1,2},{2,3},{3,4},{4,5},{5,6},{6,7},{7,8},{8,9},{9,10},{10,1... | collective-permute-start | bytes 786440 | tf_op jit(solution)/shard_map/ppermute | solution.py:17
  91.8 4.8 %collective-permute-start.2 = (f32[320,641]{1,0:T(8,128)S(1)}, f32[320,641]{1,0:T(8,128)S(1)}, u32[]{:S(2)}, u32[]{:S(2)}) collective-permute-start(f32[320,641]{1,0:T(8,128)S(1)} %fusion.34), channel_id=1, source_target_pairs={{0,1},{1,0},{2,3},{3,2},{4,5},{5,4},{6,7},{7,6},{8,9},{9,8},{10,11... | collective-permute-start | bytes 2461448 | tf_op jit(solution)/shard_map/ppermute | solution.py:55
  96.7 17.3 %collective-permute-start.5 = (f32[80,641]{1,0:T(8,128)S(1)}, f32[80,641]{1,0:T(8,128)S(1)}, u32[]{:S(2)}, u32[]{:S(2)}) collective-permute-start(f32[80,641]{1,0:T(8,128)S(1)} %get-tuple-element.26), channel_id=1, source_target_pairs={{0,6},{1,7},{2,0},{3,1},{4,2},{5,3},{6,4},{7,5},{8,14},{9,15},{10,... | collective-permute-start | bytes 615368 | tf_op jit(solution)/shard_map/ppermute | solution.py:55
  103.5 10.6 %collective-permute-start.4 = (f32[80,641]{1,0:T(8,128)S(1)}, f32[80,641]{1,0:T(8,128)S(1)}, u32[]{:S(2)}, u32[]{:S(2)}) collective-permute-start(f32[80,641]{1,0:T(8,128)S(1)} %get-tuple-element.27), channel_id=1, source_target_pairs={{0,4},{1,5},{2,6},{3,7},{4,0},{5,1},{6,2},{7,3},{8,12},{9,13},{10,... | collective-permute-start | bytes 615368 | tf_op jit(solution)/shard_map/ppermute | solution.py:55
  103.5 14.1 %collective-permute-start.3 = (f32[80,641]{1,0:T(8,128)S(1)}, f32[80,641]{1,0:T(8,128)S(1)}, u32[]{:S(2)}, u32[]{:S(2)}) collective-permute-start(f32[80,641]{1,0:T(8,128)S(1)} %get-tuple-element.25), channel_id=1, source_target_pairs={{0,2},{1,3},{2,4},{3,5},{4,6},{5,7},{6,0},{7,1},{8,10},{9,11},{10,... | collective-permute-start | bytes 615368 | tf_op jit(solution)/shard_map/ppermute | solution.py:55
  119.3 5.4 %collective-permute-start.8 = (f32[20,641]{1,0:T(8,128)S(1)}, f32[20,641]{1,0:T(8,128)S(1)}, u32[]{:S(2)}, u32[]{:S(2)}) collective-permute-start(f32[20,641]{1,0:T(8,128)S(1)} %get-tuple-element.33), channel_id=1, source_target_pairs={{0,24},{1,25},{2,26},{3,27},{4,28},{5,29},{6,30},{7,31},{8,0},{9,1... | collective-permute-start | bytes 153848 | tf_op jit(solution)/shard_map/ppermute | solution.py:55
  119.4 5.4 %collective-permute-start.7 = (f32[20,641]{1,0:T(8,128)S(1)}, f32[20,641]{1,0:T(8,128)S(1)}, u32[]{:S(2)}, u32[]{:S(2)}) collective-permute-start(f32[20,641]{1,0:T(8,128)S(1)} %get-tuple-element.34), channel_id=1, source_target_pairs={{0,16},{1,17},{2,18},{3,19},{4,20},{5,21},{6,22},{7,23},{8,24},{9,... | collective-permute-start | bytes 153848 | tf_op jit(solution)/shard_map/ppermute | solution.py:55
  122.5 4.4 %collective-permute-start.6 = (f32[20,641]{1,0:T(8,128)S(1)}, f32[20,641]{1,0:T(8,128)S(1)}, u32[]{:S(2)}, u32[]{:S(2)}) collective-permute-start(f32[20,641]{1,0:T(8,128)S(1)} %get-tuple-element.32), channel_id=1, source_target_pairs={{0,8},{1,9},{2,10},{3,11},{4,12},{5,13},{6,14},{7,15},{8,16},{9,17... | collective-permute-start | bytes 153848 | tf_op jit(solution)/shard_map/ppermute | solution.py:55
  128.4 7.6 %collective-permute-start.11 = (f32[5,641]{1,0:T(8,128)S(1)}, f32[5,641]{1,0:T(8,128)S(1)}, u32[]{:S(2)}, u32[]{:S(2)}) collective-permute-start(f32[5,641]{1,0:T(8,128)S(1)} %get-tuple-element.40), channel_id=1, source_target_pairs={{0,96},{1,97},{2,98},{3,99},{4,100},{5,101},{6,102},{7,103},{8,104... | collective-permute-start | bytes 38468 | tf_op jit(solution)/shard_map/ppermute | solution.py:55
  132.3 4.2 %collective-permute-start.10 = (f32[5,641]{1,0:T(8,128)S(1)}, f32[5,641]{1,0:T(8,128)S(1)}, u32[]{:S(2)}, u32[]{:S(2)}) collective-permute-start(f32[5,641]{1,0:T(8,128)S(1)} %get-tuple-element.41), channel_id=1, source_target_pairs={{0,64},{1,65},{2,66},{3,67},{4,68},{5,69},{6,70},{7,71},{8,72},{9,... | collective-permute-start | bytes 38468 | tf_op jit(solution)/shard_map/ppermute | solution.py:55
  132.3 4.2 %collective-permute-start.9 = (f32[5,641]{1,0:T(8,128)S(1)}, f32[5,641]{1,0:T(8,128)S(1)}, u32[]{:S(2)}, u32[]{:S(2)}) collective-permute-start(f32[5,641]{1,0:T(8,128)S(1)} %get-tuple-element.39), channel_id=1, source_target_pairs={{0,32},{1,33},{2,34},{3,35},{4,36},{5,37},{6,38},{7,39},{8,40},{9,... | collective-permute-start | bytes 38468 | tf_op jit(solution)/shard_map/ppermute | solution.py:55
  136.5 9.3 %copy-start.2 = (bf16[10,64,2050]{2,1,0:T(8,128)(2,1)S(1)}, bf16[10,64,2050]{2,1,0:T(8,128)(2,1)}, u32[]{:S(2)}) copy-start(bf16[10,64,2050]{2,1,0:T(8,128)(2,1)} %copy-done.1) | copy-start | bytes 7872004
  136.5 6.3 %collective-permute-start.12 = (f32[5,641]{1,0:T(8,128)S(1)}, f32[5,641]{1,0:T(8,128)S(1)}, u32[]{:S(2)}, u32[]{:S(2)}) collective-permute-start(f32[5,641]{1,0:T(8,128)S(1)} %fusion.65), channel_id=1, source_target_pairs={{0,96},{1,97},{2,98},{3,99},{4,100},{5,101},{6,102},{7,103},{8,104... | collective-permute-start | bytes 38468 | tf_op jit(solution)/shard_map/ppermute | solution.py:59
  138.2 4.6 %collective-permute-start.13 = (f32[5,641]{1,0:T(8,128)S(1)}, f32[5,641]{1,0:T(8,128)S(1)}, u32[]{:S(2)}, u32[]{:S(2)}) collective-permute-start(f32[5,641]{1,0:T(8,128)S(1)} %fusion.65), channel_id=1, source_target_pairs={{0,64},{1,65},{2,66},{3,67},{4,68},{5,69},{6,70},{7,71},{8,72},{9,... | collective-permute-start | bytes 38468 | tf_op jit(solution)/shard_map/ppermute | solution.py:59
  139.9 3.9 %collective-permute-start.14 = (f32[5,641]{1,0:T(8,128)S(1)}, f32[5,641]{1,0:T(8,128)S(1)}, u32[]{:S(2)}, u32[]{:S(2)}) collective-permute-start(f32[5,641]{1,0:T(8,128)S(1)} %fusion.65), channel_id=1, source_target_pairs={{0,32},{1,33},{2,34},{3,35},{4,36},{5,37},{6,38},{7,39},{8,40},{9,... | collective-permute-start | bytes 38468 | tf_op jit(solution)/shard_map/ppermute | solution.py:59
  143.9 3.6 %collective-permute-start.15 = (f32[20,641]{1,0:T(8,128)S(1)}, f32[20,641]{1,0:T(8,128)S(1)}, u32[]{:S(2)}, u32[]{:S(2)}) collective-permute-start(f32[20,641]{1,0:T(8,128)S(1)} %pad_maximum_fusion.7), channel_id=1, source_target_pairs={{0,24},{1,25},{2,26},{3,27},{4,28},{5,29},{6,30},{7,31},{8,0},{9,1... | collective-permute-start | bytes 153848 | tf_op jit(solution)/shard_map/ppermute | solution.py:59
  144.4 4.7 %collective-permute-start.16 = (f32[20,641]{1,0:T(8,128)S(1)}, f32[20,641]{1,0:T(8,128)S(1)}, u32[]{:S(2)}, u32[]{:S(2)}) collective-permute-start(f32[20,641]{1,0:T(8,128)S(1)} %pad_maximum_fusion.7), channel_id=1, source_target_pairs={{0,16},{1,17},{2,18},{3,19},{4,20},{5,21},{6,22},{7,23},{8,24},{9,... | collective-permute-start | bytes 153848 | tf_op jit(solution)/shard_map/ppermute | solution.py:59
  145.7 4.4 %collective-permute-start.17 = (f32[20,641]{1,0:T(8,128)S(1)}, f32[20,641]{1,0:T(8,128)S(1)}, u32[]{:S(2)}, u32[]{:S(2)}) collective-permute-start(f32[20,641]{1,0:T(8,128)S(1)} %pad_maximum_fusion.7), channel_id=1, source_target_pairs={{0,8},{1,9},{2,10},{3,11},{4,12},{5,13},{6,14},{7,15},{8,16},{9,17... | collective-permute-start | bytes 153848 | tf_op jit(solution)/shard_map/ppermute | solution.py:59
  150.2 5.4 %collective-permute-start.18 = (f32[80,641]{1,0:T(8,128)S(1)}, f32[80,641]{1,0:T(8,128)S(1)}, u32[]{:S(2)}, u32[]{:S(2)}) collective-permute-start(f32[80,641]{1,0:T(8,128)S(1)} %pad_maximum_fusion.6), channel_id=1, source_target_pairs={{0,6},{1,7},{2,0},{3,1},{4,2},{5,3},{6,4},{7,5},{8,14},{9,15},{10,... | collective-permute-start | bytes 615368 | tf_op jit(solution)/shard_map/ppermute | solution.py:59
  150.4 6.7 %collective-permute-start.19 = (f32[80,641]{1,0:T(8,128)S(1)}, f32[80,641]{1,0:T(8,128)S(1)}, u32[]{:S(2)}, u32[]{:S(2)}) collective-permute-start(f32[80,641]{1,0:T(8,128)S(1)} %pad_maximum_fusion.6), channel_id=1, source_target_pairs={{0,4},{1,5},{2,6},{3,7},{4,0},{5,1},{6,2},{7,3},{8,12},{9,13},{10,... | collective-permute-start | bytes 615368 | tf_op jit(solution)/shard_map/ppermute | solution.py:59
  151.2 8.3 %collective-permute-start.20 = (f32[80,641]{1,0:T(8,128)S(1)}, f32[80,641]{1,0:T(8,128)S(1)}, u32[]{:S(2)}, u32[]{:S(2)}) collective-permute-start(f32[80,641]{1,0:T(8,128)S(1)} %pad_maximum_fusion.6), channel_id=1, source_target_pairs={{0,2},{1,3},{2,4},{3,5},{4,6},{5,7},{6,0},{7,1},{8,10},{9,11},{10,... | collective-permute-start | bytes 615368 | tf_op jit(solution)/shard_map/ppermute | solution.py:59
  154.7 13.5 %copy-start.6 = (bf16[1,64,8,2048]{3,1,2,0:T(8,128)(2,1)S(1)}, bf16[1,64,8,2048]{3,1,2,0:T(8,128)(2,1)}, u32[]{:S(2)}) copy-start(bf16[1,64,8,2048]{3,1,2,0:T(8,128)(2,1)} %copy-done.5) | copy-start | bytes 6291460
  154.7 13.5 %copy-start.17 = (bf16[1,64,2048]{2,1,0:T(8,128)(2,1)S(1)}, bf16[1,64,2048]{2,1,0:T(8,128)(2,1)}, u32[]{:S(2)}) copy-start(bf16[1,64,2048]{2,1,0:T(8,128)(2,1)} %copy-done.16) | copy-start | bytes 786436
  159.8 11.6 %collective-permute-start.21 = (f32[320,641]{1,0:T(8,128)S(1)}, f32[320,641]{1,0:T(8,128)S(1)}, u32[]{:S(2)}, u32[]{:S(2)}) collective-permute-start(f32[320,641]{1,0:T(8,128)S(1)} %pad_maximum_fusion.4), channel_id=1, source_target_pairs={{0,1},{1,0},{2,3},{3,2},{4,5},{5,4},{6,7},{7,6},{8,9},{9,8},{10,11... | collective-permute-start | bytes 2461448 | tf_op jit(solution)/shard_map/ppermute | solution.py:59
  174.4 6.4 %copy-start.15 = (f32[576,576]{1,0:T(8,128)S(1)}, f32[576,576]{1,0:T(8,128)}, u32[]{:S(2)}) copy-start(f32[576,576]{1,0:T(8,128)} %get-tuple-element.10) | copy-start | bytes 3981316
  222.0 6.2 %copy-start.14 = (f32[576,576]{1,0:T(8,128)S(1)}, f32[576,576]{1,0:T(8,128)}, u32[]{:S(2)}) copy-start(f32[576,576]{1,0:T(8,128)} %fusion.87) | copy-start | bytes 3981316
  (11 other events, 27.0 us)
where the time goes:
time: 266 us; the launch traced here: 263 us
  matrix products  104 us (39%)
  local copies, waits for them, and re-layouts  60 us (23%)
  starting transfers between devices  43.6 us (16%)
  other arithmetic  30.8 us (12%)
  waiting for transfers between devices  21.7 us (8%)
    unnamed x59, local copies, waits for them, and re-layouts  51.2 us
    dot_general x1, matrix products, on_device(): lax.dot_general(stacked, stacked, contract_pixels, preferred_element_type...  22.7 us
    dot_general x4, matrix products, on_device(): iter_y = jnp.dot(factor, iter_y, precision=highest)  20.2 us
    dot_general x4, matrix products, on_device(): factor = 0.5 * (3.0 * identity - jnp.dot(iter_z, iter_y, precision=highest))  18.9 us
    dot_general x4, matrix products, on_device(): iter_z = jnp.dot(factor, iter_z, precision=highest)  18.6 us
    ppermute x10, starting transfers between devices, tree_psum(): block = block + lax.ppermute(send, axes, pairs)  15.8 us
    ppermute x10, starting transfers between devices, tree_psum(): pieces = [block] + [lax.ppermute(block, axes, pairs) for pairs in shifts]  15.6 us
    unnamed x6, other arithmetic  13.3 us
  transfers between devices with their start and end apart: 24, of which 10 were waited for; matrix products, arithmetic and copies ran while one was open for 13% of the time, Pallas kernels for 0%

commit v1 on v0

--- a/solution.py
+++ b/solution.py
@@ -22,15 +22,9 @@
     return block
 
 
-def tap_stack(padded, strip_rows, img_width, flipped):
-    shifted = [padded[:, :, first_col : first_col + img_width] for first_col in range(3)]
-    pieces = []
-    for tap_row in range(3):
-        for tap_col in range(3):
-            first_row = 2 - tap_row if flipped else tap_row
-            first_col = 2 - tap_col if flipped else tap_col
-            pieces.append(shifted[first_col][first_row : first_row + strip_rows])
-    return pieces
+def column_taps(padded, img_width, flipped):
+    order = (2, 1, 0) if flipped else (0, 1, 2)
+    return jnp.concatenate([padded[:, :, first : first + img_width] for first in order], axis=1)
 
 
 def tree_psum(block, axes, levels):
@@ -97,12 +91,40 @@
     gpadded = jnp.pad(gframed, ((0, 0), (0, 0), (1, 1)))
     contract_pixels = (((0, 2), (0, 2)), ((), ()))
 
-    stacked = jnp.concatenate(tap_stack(padded, strip_rows, img_width, False) + [grad_first], axis=1)
-    moments = lax.dot_general(
-        stacked, stacked, contract_pixels, preferred_element_type=jnp.float32
+    taps = column_taps(padded, img_width, False)
+    band = 3 * channels
+
+    def block_of(first, second):
+        return lax.dot_general(
+            taps[first : first + strip_rows],
+            taps[second : second + strip_rows],
+            contract_pixels,
+            preferred_element_type=jnp.float32,
+        )
+
+    upper = {(i, j): block_of(i, j) for i in range(3) for j in range(i, 3)}
+    gram_rows = [
+        jnp.concatenate([upper[(i, j)] if j >= i else upper[(j, i)].T for j in range(3)], axis=1)
+        for i in range(3)
+    ]
+    gram_part = jnp.concatenate(gram_rows, axis=0)
+    cross_part = jnp.concatenate(
+        [
+            lax.dot_general(
+                taps[i : i + strip_rows], grad_first, contract_pixels, preferred_element_type=jnp.float32
+            )
+            for i in range(3)
+        ],
+        axis=0,
     )
-    sums = jnp.sum(stacked, axis=(0, 2), dtype=jnp.float32)
-    local = jnp.concatenate([moments, sums[:, None]], axis=1)
+    row_sums = jnp.sum(taps, axis=2, dtype=jnp.float32)
+    patch_part = jnp.concatenate([jnp.sum(row_sums[i : i + strip_rows], axis=0) for i in range(3)])
+    grad_part = jnp.sum(grad_first, axis=(0, 2), dtype=jnp.float32)
+    top = jnp.concatenate([gram_part, cross_part, patch_part[:, None]], axis=1)
+    bottom = jnp.concatenate(
+        [jnp.zeros((channels, patch_dim + channels), jnp.float32), grad_part[:, None]], axis=1
+    )
+    local = jnp.concatenate([top, bottom], axis=0)
     world = lax.axis_size("dp") * lax.axis_size("rows")
     total = tree_psum(local, ("dp", "rows"), physical_levels(world))
 
@@ -132,17 +154,24 @@
         jnp.dot(inv_root.T, cross_total - jnp.outer(mean_vec, grad_sum), precision=highest)
         / pixels
     )
-    back_w = mixing_b.reshape(9, channels, channels).transpose(1, 0, 2).reshape(channels, patch_dim)
-    contract_taps = (((0,), (1,)), ((), ()))
-    out_rows = lax.dot_general(
-        mixing_b, stacked[:, :patch_dim], contract_taps, preferred_element_type=jnp.float32
-    )
-    out_buffer = (out_rows + bias_shift[:, None, None]).astype(jnp.bfloat16)
-    gstacked = jnp.concatenate(tap_stack(gpadded, strip_rows, img_width, True), axis=1)
+    contract_band = (((0,), (1,)), ((), ()))
+    forward_bands = mixing_b.reshape(3, band, channels)
+    out_rows = bias_shift[:, None, None]
+    for i in range(3):
+        out_rows = out_rows + lax.dot_general(
+            forward_bands[i], taps[i : i + strip_rows], contract_band, preferred_element_type=jnp.float32
+        )
+    out_buffer = out_rows.astype(jnp.bfloat16)
+    gtaps = column_taps(gpadded, img_width, True)
+    flipped = mixing_b.reshape(3, 3, channels, channels)[::-1]
+    back_bands = flipped.transpose(0, 2, 1, 3).reshape(3, channels, band)
     contract_back = (((1,), (1,)), ((), ()))
-    back_rows = lax.dot_general(
-        back_w, gstacked, contract_back, preferred_element_type=jnp.float32
-    )
+    back_rows = None
+    for i in range(3):
+        term = lax.dot_general(
+            back_bands[i], gtaps[i : i + strip_rows], contract_back, preferred_element_type=jnp.float32
+        )
+        back_rows = term if back_rows is None else back_rows + term
     back_buffer = back_rows.astype(jnp.bfloat16)
     return (out_buffer[None], back_buffer[None], grad_w)
 

time: 266 us -> 238 us (0.89)
  local copies, waits for them, and re-layouts: 60 us -> 16.8 us
  waiting for transfers between devices: 21.7 us -> 39.4 us
  matrix products: 104 us -> 120 us
  other arithmetic: 30.8 us -> 18.1 us
  starting transfers between devices: 43.6 us -> 36 us
    unnamed x59 -> x22, local copies, waits for them, and re-layouts: 51.2 us -> 11.7 us
    dot_general x3 -> x15, matrix products: 42.9 us -> 57.2 us  [the longest x3 18.8 us: on_device(): lax.dot_general(back_bands[i], gtaps[i:i + strip_rows], contract_back, pr...]
    unnamed x6 -> x1, other arithmetic: 13.3 us -> 0.01 us
    ppermute x10, waiting for transfers between devices: 13.1 us -> 21.8 us  [tree_psum(): block = block + lax.ppermute(send, axes, pairs)]
    ppermute x10, starting transfers between devices: 15.6 us -> 7.02 us  [tree_psum(): pieces = [block] + [lax.ppermute(block, axes, pairs) for pairs in shifts]]
    ppermute x10, waiting for transfers between devices: 8.52 us -> 16.1 us  [tree_psum(): pieces = [block] + [lax.ppermute(block, axes, pairs) for pairs in shifts]]
    concatenate x0 -> x3, other arithmetic: none -> 5.8 us  [the longest x1 4.01 us: column_taps(): jnp.concatenate([padded[:, :, first:first + img_width] for first in order...]
    concatenate x3 -> x0, local copies, waits for them, and re-layouts: 4.67 us -> none  [the longest x1 2.8 us: on_device(): jnp.concatenate(tap_stack(padded, strip_rows, img_width, False) + [grad_f...]
  transfers between devices with their start and end apart: 24 -> 24, of which waited for: 10 -> 13; matrix products, arithmetic and copies ran while one was open for 13% -> 6% of each run, Pallas kernels for 0% -> 0%
where the time goes in v1:
time: 238 us; the launch traced here: 233 us
  matrix products  120 us (50%)
  waiting for transfers between devices  39.4 us (17%)
  starting transfers between devices  36 us (15%)
  other arithmetic  18.1 us (8%)
  local copies, waits for them, and re-layouts  16.8 us (7%)
  between operations  2.84 us (1%)
    ppermute x10, waiting for transfers between devices, tree_psum(): block = block + lax.ppermute(send, axes, pairs)  21.8 us
    dot_general x4, matrix products, on_device(): iter_y = jnp.dot(factor, iter_y, precision=highest)  20.4 us
    dot_general x4, matrix products, on_device(): iter_z = jnp.dot(factor, iter_z, precision=highest)  19.9 us
    dot_general x4, matrix products, on_device(): factor = 0.5 * (3.0 * identity - jnp.dot(iter_z, iter_y, precision=highest))  18.9 us
    dot_general x3, matrix products, on_device(): lax.dot_general(back_bands[i], gtaps[i:i + strip_rows], contract_back, pr...  18.8 us
    ppermute x10, waiting for transfers between devices, tree_psum(): pieces = [block] + [lax.ppermute(block, axes, pairs) for pairs in shifts]  16.1 us
    ppermute x10, starting transfers between devices, tree_psum(): block = block + lax.ppermute(send, axes, pairs)  15.2 us
    dot_general x3, matrix products, on_device(): lax.dot_general(forward_bands[i], taps[i:i + strip_rows], contract_band,...  13.3 us
  transfers between devices with their start and end apart: 24, of which 13 were waited for; matrix products, arithmetic and copies ran while one was open for 6% of the time, Pallas kernels for 0%

profile of v1, /device:TPU:1, one launch (start us, length us, event | category | flops | bytes accessed | tf_op | source)
XLA Modules:
  0.0 233.4 jit_solution(7617475751984264497)
XLA Ops:
  3.5 3.3 %collective-permute-start.1 = (bf16[1,64,2048]{2,1,0:T(8,128)(2,1)S(1)}, bf16[1,64,2048]{2,1,0:T(8,128)(2,1)S(1)}, u32[]{:S(2)}, u32[]{:S(2)}) collective-permute-start(bf16[1,64,2048]{2,1,0:T(8,128)(2,1)S(1)} %get-tuple-element.26), channel_id=1, source_target_pairs={{1,0},{2,1},{3,2},{4,3},{5,4},{6,5},{7,6},{8,7},{9,8},{10,9},{11,1... | collective-permute-start | bytes 786440 | tf_op jit(solution)/shard_map/ppermute | solution.py:20
  18.4 3.5 %convolution_bitcast_fusion = f32[192,64]{1,0:T(8,128)S(1)} fusion(bf16[10,192,2048]{2,1,0:T(8,128)(2,1)S(1)} %get-tuple-element.18, bf16[1,64,8,2048]{3,2,1,0:T(8,128)(2,1)S(1)} %copy-done.2), kind=kOutput, calls=%fused_computation.74 | convolution fusion | flops 402653184 | bytes 10010624 | tf_op jit(solution)/shard_map/dot_general | solution.py:113
  21.9 4.2 %convolution_bitcast_fusion.1 = f32[192,64]{1,0:T(8,128)} fusion(bf16[10,192,2048]{2,1,0:T(8,128)(2,1)S(1)} %get-tuple-element.18, bf16[1,64,8,2048]{3,2,1,0:T(8,128)(2,1)S(1)} %copy-done.2), kind=kOutput, calls=%fused_computation.75 | convolution fusion | flops 402653184 | bytes 10010624 | tf_op jit(solution)/shard_map/dot_general | solution.py:113
  26.1 4.1 %convolution_bitcast_fusion.2 = f32[192,64]{1,0:T(8,128)} fusion(bf16[10,192,2048]{2,1,0:T(8,128)(2,1)S(1)} %get-tuple-element.18, bf16[1,64,8,2048]{3,2,1,0:T(8,128)(2,1)S(1)} %copy-done.2), kind=kOutput, calls=%fused_computation.76 | convolution fusion | flops 402653184 | bytes 10010624 | tf_op jit(solution)/shard_map/dot_general | solution.py:113
  50.8 4.6 %collective-permute-start.5 = (f32[80,641]{1,0:T(8,128)S(1)}, f32[80,641]{1,0:T(8,128)S(1)}, u32[]{:S(2)}, u32[]{:S(2)}) collective-permute-start(f32[80,641]{1,0:T(8,128)S(1)} %get-tuple-element.34), channel_id=1, source_target_pairs={{0,6},{1,7},{2,0},{3,1},{4,2},{5,3},{6,4},{7,5},{8,14},{9,15},{10,... | collective-permute-start | bytes 615368 | tf_op jit(solution)/shard_map/ppermute | solution.py:49
  56.1 9.8 %collective-permute-done.5 = f32[80,641]{1,0:T(8,128)S(1)} collective-permute-done((f32[80,641]{1,0:T(8,128)S(1)}, f32[80,641]{1,0:T(8,128)S(1)}, u32[]{:S(2)}, u32[]{:S(2)}) %collective-permute-start.5) | collective-permute-done | bytes 205152 | tf_op jit(solution)/shard_map/ppermute | solution.py:49
  65.9 3.6 %collective-permute-done.3 = f32[80,641]{1,0:T(8,128)S(1)} collective-permute-done((f32[80,641]{1,0:T(8,128)S(1)}, f32[80,641]{1,0:T(8,128)S(1)}, u32[]{:S(2)}, u32[]{:S(2)}) %collective-permute-start.3) | collective-permute-done | bytes 205152 | tf_op jit(solution)/shard_map/ppermute | solution.py:49
  69.6 4.4 %collective-permute-start.8 = (f32[20,641]{1,0:T(8,128)S(1)}, f32[20,641]{1,0:T(8,128)S(1)}, u32[]{:S(2)}, u32[]{:S(2)}) collective-permute-start(f32[20,641]{1,0:T(8,128)S(1)} %get-tuple-element.41), channel_id=1, source_target_pairs={{0,24},{1,25},{2,26},{3,27},{4,28},{5,29},{6,30},{7,31},{8,0},{9,1... | collective-permute-start | bytes 153848 | tf_op jit(solution)/shard_map/ppermute | solution.py:49
  80.0 3.9 %collective-permute-start.11 = (f32[5,641]{1,0:T(8,128)S(1)}, f32[5,641]{1,0:T(8,128)S(1)}, u32[]{:S(2)}, u32[]{:S(2)}) collective-permute-start(f32[5,641]{1,0:T(8,128)S(1)} %get-tuple-element.51), channel_id=1, source_target_pairs={{0,96},{1,97},{2,98},{3,99},{4,100},{5,101},{6,102},{7,103},{8,104... | collective-permute-start | bytes 38468 | tf_op jit(solution)/shard_map/ppermute | solution.py:49
  91.3 5.4 %collective-permute-start.23 = (bf16[1,64,2048]{2,1,0:T(8,128)(2,1)S(1)}, bf16[1,64,2048]{2,1,0:T(8,128)(2,1)S(1)}, u32[]{:S(2)}, u32[]{:S(2)}) collective-permute-start(bf16[1,64,2048]{2,1,0:T(8,128)(2,1)S(1)} %get-tuple-element.24), channel_id=1, source_target_pairs={{1,0},{2,1},{3,2},{4,3},{5,4},{6,5},{7,6},{8,7},{9,8},{10,9},{11,1... | collective-permute-start | bytes 786440 | tf_op jit(solution)/shard_map/ppermute | solution.py:20
  103.7 4.2 %collective-permute-done.16 = f32[20,641]{1,0:T(8,128)S(1)} collective-permute-done((f32[20,641]{1,0:T(8,128)S(1)}, f32[20,641]{1,0:T(8,128)S(1)}, u32[]{:S(2)}, u32[]{:S(2)}) %collective-permute-start.16) | collective-permute-done | bytes 51312 | tf_op jit(solution)/shard_map/ppermute | solution.py:53
  111.0 4.0 %collective-permute-done.18 = f32[80,641]{1,0:T(8,128)S(1)} collective-permute-done((f32[80,641]{1,0:T(8,128)S(1)}, f32[80,641]{1,0:T(8,128)S(1)}, u32[]{:S(2)}, u32[]{:S(2)}) %collective-permute-start.18) | collective-permute-done | bytes 205152 | tf_op jit(solution)/shard_map/ppermute | solution.py:53
  116.9 6.0 %collective-permute-done.20 = f32[80,641]{1,0:T(8,128)S(1)} collective-permute-done((f32[80,641]{1,0:T(8,128)S(1)}, f32[80,641]{1,0:T(8,128)S(1)}, u32[]{:S(2)}, u32[]{:S(2)}) %collective-permute-start.20) | collective-permute-done | bytes 205152 | tf_op jit(solution)/shard_map/ppermute | solution.py:53
  123.7 4.0 %pad_maximum_fusion.1 = bf16[10,192,2048]{2,1,0:T(8,128)(2,1)} fusion(bf16[10,64,2048]{2,1,0:T(8,128)(2,1)S(1)} %get-tuple-element.20, bf16[1,64,2048]{2,1,0:T(8,128)(2,1)S(1)} %collective-permute-done.23, bf16[8,64,2048]{2,1,0:T(8,128)(2,1)S(1)} %bitcast.148, bf16[1,64,2048]{2,1,0:T(8,128)(2,1)S(1)} %collective-permute-done.22, ...), kind=kLoop, calls=%fused_computation.4 | loop fusion | flops 39321600 | bytes 15728640 | tf_op jit(solution)/shard_map/concatenate | solution.py:27
  130.8 6.3 %fusion.47 = f32[576,576]{1,0:T(8,128)S(1)} fusion(f32[576,576]{1,0:T(8,128)} %get-tuple-element.16, f32[]{:T(128)S(6)} %sqrt.6), kind=kOutput, calls=%fused_computation.65 | convolution fusion | flops 2295226368 | bytes 2654212 | tf_op jit(solution)/shard_map/dot_general | solution.py:142
  137.1 4.2 %fusion.37 = f32[576,576]{1,0:T(8,128)S(1)} fusion(f32[576,576]{1,0:T(8,128)S(1)} %fusion.47, f32[576,576]{1,0:T(8,128)S(1)} %copy-done.5, f32[]{:T(128)S(6)} %sqrt.6), kind=kOutput, calls=%fused_computation.56 | convolution fusion | flops 2296221696 | bytes 3981316 | tf_op jit(solution)/shard_map/dot_general | solution.py:145
  141.4 4.7 %fusion.43 = f32[576,576]{1,0:T(8,128)S(1)} fusion(f32[576,576]{1,0:T(8,128)S(1)} %fusion.37, f32[576,576]{1,0:T(8,128)S(1)} %copy-done.5, f32[]{:T(128)S(6)} %sqrt.6), kind=kOutput, calls=%fused_computation.63 | convolution fusion | flops 2294894592 | bytes 3981316 | tf_op jit(solution)/shard_map/dot_general | solution.py:148
  146.1 4.2 %fusion.120 = f32[576,576]{1,0:T(8,128)S(1)} fusion(f32[576,576]{1,0:T(8,128)S(1)} %fusion.37, f32[576,576]{1,0:T(8,128)S(1)} %fusion.47), kind=kOutput, calls=%fused_computation.165 | convolution fusion | flops 2293235712 | bytes 3981312 | tf_op jit(solution)/shard_map/dot_general | solution.py:147
  150.3 4.2 %fusion.38 = f32[576,576]{1,0:T(8,128)S(1)} fusion(f32[576,576]{1,0:T(8,128)S(1)} %fusion.43, f32[576,576]{1,0:T(8,128)S(1)} %fusion.120), kind=kOutput, calls=%fused_computation.57 | convolution fusion | flops 2294562816 | bytes 3981312 | tf_op jit(solution)/shard_map/dot_general | solution.py:145
  154.6 4.2 %fusion.121 = f32[576,576]{1,0:T(8,128)S(1)} fusion(f32[576,576]{1,0:T(8,128)S(1)} %fusion.38, f32[576,576]{1,0:T(8,128)S(1)} %fusion.43), kind=kOutput, calls=%fused_computation.166 | convolution fusion | flops 2293235712 | bytes 3981312 | tf_op jit(solution)/shard_map/dot_general | solution.py:148
  158.8 4.4 %fusion.122 = f32[576,576]{1,0:T(8,128)S(1)} fusion(f32[576,576]{1,0:T(8,128)S(1)} %fusion.38, f32[576,576]{1,0:T(8,128)S(1)} %fusion.120), kind=kOutput, calls=%fused_computation.167 | convolution fusion | flops 2293235712 | bytes 3981312 | tf_op jit(solution)/shard_map/dot_general | solution.py:147
  163.2 4.2 %fusion.39 = f32[576,576]{1,0:T(8,128)S(1)} fusion(f32[576,576]{1,0:T(8,128)S(1)} %fusion.121, f32[576,576]{1,0:T(8,128)S(1)} %fusion.122), kind=kOutput, calls=%fused_computation.58 | convolution fusion | flops 2294562816 | bytes 3981312 | tf_op jit(solution)/shard_map/dot_general | solution.py:145
  167.4 5.2 %fusion.123 = f32[576,576]{1,0:T(8,128)} fusion(f32[576,576]{1,0:T(8,128)S(1)} %fusion.39, f32[576,576]{1,0:T(8,128)S(1)} %fusion.121), kind=kOutput, calls=%fused_computation.168 | convolution fusion | flops 2293235712 | bytes 3981312 | tf_op jit(solution)/shard_map/dot_general | solution.py:148
  172.7 5.5 %fusion.124 = f32[576,576]{1,0:T(8,128)} fusion(f32[576,576]{1,0:T(8,128)S(1)} %fusion.39, f32[576,576]{1,0:T(8,128)S(1)} %fusion.122), kind=kOutput, calls=%fused_computation.169 | convolution fusion | flops 2293235712 | bytes 3981312 | tf_op jit(solution)/shard_map/dot_general | solution.py:147
  178.2 6.2 %fusion.125 = f32[576,576]{1,0:T(8,128)S(1)} fusion(f32[576,576]{1,0:T(8,128)} %fusion.123, f32[576,576]{1,0:T(8,128)} %fusion.124), kind=kOutput, calls=%fused_computation.170 | convolution fusion | flops 2293235712 | bytes 3981312 | tf_op jit(solution)/shard_map/dot_general | solution.py:145
  184.4 5.8 %fusion.51 = f32[576,576]{1,0:T(8,128)S(1)} fusion(f32[576,576]{1,0:T(8,128)} %fusion.123, f32[576,576]{1,0:T(8,128)S(1)} %fusion.125, f32[]{:T(128)S(6)} %sqrt.7), kind=kOutput, calls=%fused_computation.66 | convolution fusion | flops 2294894592 | bytes 3981316 | tf_op jit(solution)/shard_map/dot_general | solution.py:148
  193.2 3.3 %fusion.11 = f32[64,8,2048]{2,0,1:T(8,128)} fusion(bf16[10,192,2048]{2,1,0:T(8,128)(2,1)S(1)} %bitcast.145, bf16[576,64]{0,1:T(8,128)(2,1)S(1)} %get-tuple-element.53), kind=kOutput, calls=%fused_computation.16 | convolution fusion | flops 402653184 | bytes 10518528 | tf_op jit(solution)/shard_map/dot_general | solution.py:161
  196.5 3.3 %fusion.7 = f32[64,8,2048]{2,0,1:T(8,128)} fusion(bf16[10,192,2048]{2,1,0:T(8,128)(2,1)S(1)} %bitcast.145, bf16[576,64]{0,1:T(8,128)(2,1)S(1)} %get-tuple-element.53), kind=kOutput, calls=%fused_computation.12 | convolution fusion | flops 402653184 | bytes 10518528 | tf_op jit(solution)/shard_map/dot_general | solution.py:161
  200.3 6.7 %fusion.28 = bf16[1,64,8,2048]{3,1,2,0:T(8,128)(2,1)S(1)} fusion(bf16[10,192,2048]{2,1,0:T(8,128)(2,1)} %copy-done.1, f32[64,8,2048]{2,0,1:T(8,128)} %fusion.11, f32[64,8,2048]{2,0,1:T(8,128)} %fusion.7, f32[64]{0:T(128)S(1)} %fusion.72, bf16[576,64]{0,1:T(8,128)(2,1)S(1)} %get-tuple-element.53), kind=kOutput, calls=%fused_computation.43 | convolution fusion | flops 406847488 | bytes 16810496 | tf_op jit(solution)/shard_map/dot_general | solution.py:161
  209.7 6.1 %fusion.4 = f32[64,8,2048]{2,0,1:T(8,128)} fusion(bf16[64,192,1]{0,1,2:T(8,128)(2,1)S(1)} %bitcast.161, bf16[10,192,2048]{2,1,0:T(8,128)(2,1)} %pad_maximum_fusion.1), kind=kOutput, calls=%fused_computation.9 | convolution fusion | flops 402653184 | bytes 10510336 | tf_op jit(solution)/shard_map/dot_general | solution.py:171
  215.8 6.1 %fusion.2 = f32[64,8,2048]{2,0,1:T(8,128)} fusion(bf16[64,192,1]{0,1,2:T(8,128)(2,1)S(1)} %bitcast.162, bf16[10,192,2048]{2,1,0:T(8,128)(2,1)} %pad_maximum_fusion.1), kind=kOutput, calls=%fused_computation.7 | convolution fusion | flops 402653184 | bytes 10510336 | tf_op jit(solution)/shard_map/dot_general | solution.py:171
  221.9 6.7 %fusion.31 = bf16[1,64,8,2048]{3,1,2,0:T(8,128)(2,1)S(1)} fusion(f32[64,8,2048]{2,0,1:T(8,128)} %fusion.4, f32[64,8,2048]{2,0,1:T(8,128)} %fusion.2, bf16[64,192,1]{0,1,2:T(8,128)(2,1)S(1)} %bitcast.160, bf16[10,192,2048]{2,1,0:T(8,128)(2,1)} %pad_maximum_fusion.1), kind=kOutput, calls=%fused_computation.44 | convolution fusion | flops 405798912 | bytes 16801792 | tf_op jit(solution)/shard_map/dot_general | solution.py:171
  (113 shorter events, 74.3 us)
Async XLA Ops:
  0.6 190.8 %copy-start = (f32[576,64]{0,1:T(8,128)S(1)}, f32[576,64]{0,1:T(8,128)}, u32[]{:S(2)}) copy-start(f32[576,64]{0,1:T(8,128)} %param.5) | copy-start | bytes 442372
  3.5 9.3 %collective-permute-start.1 = (bf16[1,64,2048]{2,1,0:T(8,128)(2,1)S(1)}, bf16[1,64,2048]{2,1,0:T(8,128)(2,1)S(1)}, u32[]{:S(2)}, u32[]{:S(2)}) collective-permute-start(bf16[1,64,2048]{2,1,0:T(8,128)(2,1)S(1)} %get-tuple-element.26), channel_id=1, source_target_pairs={{1,0},{2,1},{3,2},{4,3},{5,4},{6,5},{7,6},{8,7},{9,8},{10,9},{11,1... | collective-permute-start | bytes 786440 | tf_op jit(solution)/shard_map/ppermute | solution.py:20
  6.8 6.4 %collective-permute-start = (bf16[1,64,2048]{2,1,0:T(8,128)(2,1)S(1)}, bf16[1,64,2048]{2,1,0:T(8,128)(2,1)S(1)}, u32[]{:S(2)}, u32[]{:S(2)}) collective-permute-start(bf16[1,64,2048]{2,1,0:T(8,128)(2,1)S(1)} %get-tuple-element.25), channel_id=1, source_target_pairs={{0,1},{1,2},{2,3},{3,4},{4,5},{5,6},{6,7},{7,8},{8,9},{9,10},{10,1... | collective-permute-start | bytes 786440 | tf_op jit(solution)/shard_map/ppermute | solution.py:17
  16.4 2.0 copy-start.2
  18.4 22.6 %copy-start.1 = (bf16[10,192,2048]{2,1,0:T(8,128)(2,1)}, bf16[10,192,2048]{2,1,0:T(8,128)(2,1)S(1)}, u32[]{:S(2)}) copy-start(bf16[10,192,2048]{2,1,0:T(8,128)(2,1)S(1)} %get-tuple-element.18) | copy-start | bytes 23592964
  46.7 2.8 %collective-permute-start.2 = (f32[320,641]{1,0:T(8,128)S(1)}, f32[320,641]{1,0:T(8,128)}, u32[]{:S(2)}, u32[]{:S(2)}) collective-permute-start(f32[320,641]{1,0:T(8,128)S(1)} %dynamic-slice_bitcast_fusion), channel_id=1, source_target_pairs={{0,1},{1,0},{2,3},{3,2},{4,5},{5,4},{6,7},{7,6},{8,9},{9,8},{10,11... | collective-permute-start | bytes 2461448 | tf_op jit(solution)/shard_map/ppermute | solution.py:49
  50.8 15.0 %collective-permute-start.5 = (f32[80,641]{1,0:T(8,128)S(1)}, f32[80,641]{1,0:T(8,128)S(1)}, u32[]{:S(2)}, u32[]{:S(2)}) collective-permute-start(f32[80,641]{1,0:T(8,128)S(1)} %get-tuple-element.34), channel_id=1, source_target_pairs={{0,6},{1,7},{2,0},{3,1},{4,2},{5,3},{6,4},{7,5},{8,14},{9,15},{10,... | collective-permute-start | bytes 615368 | tf_op jit(solution)/shard_map/ppermute | solution.py:49
  55.4 10.4 %collective-permute-start.4 = (f32[80,641]{1,0:T(8,128)S(1)}, f32[80,641]{1,0:T(8,128)S(1)}, u32[]{:S(2)}, u32[]{:S(2)}) collective-permute-start(f32[80,641]{1,0:T(8,128)S(1)} %get-tuple-element.35), channel_id=1, source_target_pairs={{0,4},{1,5},{2,6},{3,7},{4,0},{5,1},{6,2},{7,3},{8,12},{9,13},{10,... | collective-permute-start | bytes 615368 | tf_op jit(solution)/shard_map/ppermute | solution.py:49
  55.5 14.1 %collective-permute-start.3 = (f32[80,641]{1,0:T(8,128)S(1)}, f32[80,641]{1,0:T(8,128)S(1)}, u32[]{:S(2)}, u32[]{:S(2)}) collective-permute-start(f32[80,641]{1,0:T(8,128)S(1)} %get-tuple-element.33), channel_id=1, source_target_pairs={{0,2},{1,3},{2,4},{3,5},{4,6},{5,7},{6,0},{7,1},{8,10},{9,11},{10,... | collective-permute-start | bytes 615368 | tf_op jit(solution)/shard_map/ppermute | solution.py:49
  69.6 6.6 %collective-permute-start.8 = (f32[20,641]{1,0:T(8,128)S(1)}, f32[20,641]{1,0:T(8,128)S(1)}, u32[]{:S(2)}, u32[]{:S(2)}) collective-permute-start(f32[20,641]{1,0:T(8,128)S(1)} %get-tuple-element.41), channel_id=1, source_target_pairs={{0,24},{1,25},{2,26},{3,27},{4,28},{5,29},{6,30},{7,31},{8,0},{9,1... | collective-permute-start | bytes 153848 | tf_op jit(solution)/shard_map/ppermute | solution.py:49
  74.1 4.8 %collective-permute-start.7 = (f32[20,641]{1,0:T(8,128)S(1)}, f32[20,641]{1,0:T(8,128)S(1)}, u32[]{:S(2)}, u32[]{:S(2)}) collective-permute-start(f32[20,641]{1,0:T(8,128)S(1)} %get-tuple-element.42), channel_id=1, source_target_pairs={{0,16},{1,17},{2,18},{3,19},{4,20},{5,21},{6,22},{7,23},{8,24},{9,... | collective-permute-start | bytes 153848 | tf_op jit(solution)/shard_map/ppermute | solution.py:49
  74.1 5.8 %collective-permute-start.6 = (f32[20,641]{1,0:T(8,128)S(1)}, f32[20,641]{1,0:T(8,128)S(1)}, u32[]{:S(2)}, u32[]{:S(2)}) collective-permute-start(f32[20,641]{1,0:T(8,128)S(1)} %get-tuple-element.40), channel_id=1, source_target_pairs={{0,8},{1,9},{2,10},{3,11},{4,12},{5,13},{6,14},{7,15},{8,16},{9,17... | collective-permute-start | bytes 153848 | tf_op jit(solution)/shard_map/ppermute | solution.py:49
  80.0 7.4 %collective-permute-start.11 = (f32[5,641]{1,0:T(8,128)S(1)}, f32[5,641]{1,0:T(8,128)S(1)}, u32[]{:S(2)}, u32[]{:S(2)}) collective-permute-start(f32[5,641]{1,0:T(8,128)S(1)} %get-tuple-element.51), channel_id=1, source_target_pairs={{0,96},{1,97},{2,98},{3,99},{4,100},{5,101},{6,102},{7,103},{8,104... | collective-permute-start | bytes 38468 | tf_op jit(solution)/shard_map/ppermute | solution.py:49
  83.8 4.3 %collective-permute-start.10 = (f32[5,641]{1,0:T(8,128)S(1)}, f32[5,641]{1,0:T(8,128)S(1)}, u32[]{:S(2)}, u32[]{:S(2)}) collective-permute-start(f32[5,641]{1,0:T(8,128)S(1)} %get-tuple-element.52), channel_id=1, source_target_pairs={{0,64},{1,65},{2,66},{3,67},{4,68},{5,69},{6,70},{7,71},{8,72},{9,... | collective-permute-start | bytes 38468 | tf_op jit(solution)/shard_map/ppermute | solution.py:49
  83.8 4.3 %collective-permute-start.9 = (f32[5,641]{1,0:T(8,128)S(1)}, f32[5,641]{1,0:T(8,128)S(1)}, u32[]{:S(2)}, u32[]{:S(2)}) collective-permute-start(f32[5,641]{1,0:T(8,128)S(1)} %get-tuple-element.50), channel_id=1, source_target_pairs={{0,32},{1,33},{2,34},{3,35},{4,36},{5,37},{6,38},{7,39},{8,40},{9,... | collective-permute-start | bytes 38468 | tf_op jit(solution)/shard_map/ppermute | solution.py:49
  88.1 10.8 %collective-permute-start.12 = (f32[5,641]{1,0:T(8,128)S(1)}, f32[5,641]{1,0:T(8,128)S(1)}, u32[]{:S(2)}, u32[]{:S(2)}) collective-permute-start(f32[5,641]{1,0:T(8,128)S(1)} %fusion.97), channel_id=1, source_target_pairs={{0,96},{1,97},{2,98},{3,99},{4,100},{5,101},{6,102},{7,103},{8,104... | collective-permute-start | bytes 38468 | tf_op jit(solution)/shard_map/ppermute | solution.py:53
  89.5 9.5 %collective-permute-start.13 = (f32[5,641]{1,0:T(8,128)S(1)}, f32[5,641]{1,0:T(8,128)S(1)}, u32[]{:S(2)}, u32[]{:S(2)}) collective-permute-start(f32[5,641]{1,0:T(8,128)S(1)} %fusion.97), channel_id=1, source_target_pairs={{0,64},{1,65},{2,66},{3,67},{4,68},{5,69},{6,70},{7,71},{8,72},{9,... | collective-permute-start | bytes 38468 | tf_op jit(solution)/shard_map/ppermute | solution.py:53
  91.3 7.7 %collective-permute-start.14 = (f32[5,641]{1,0:T(8,128)S(1)}, f32[5,641]{1,0:T(8,128)S(1)}, u32[]{:S(2)}, u32[]{:S(2)}) collective-permute-start(f32[5,641]{1,0:T(8,128)S(1)} %fusion.97), channel_id=1, source_target_pairs={{0,32},{1,33},{2,34},{3,35},{4,36},{5,37},{6,38},{7,39},{8,40},{9,... | collective-permute-start | bytes 38468 | tf_op jit(solution)/shard_map/ppermute | solution.py:53
  91.3 9.5 %collective-permute-start.23 = (bf16[1,64,2048]{2,1,0:T(8,128)(2,1)S(1)}, bf16[1,64,2048]{2,1,0:T(8,128)(2,1)S(1)}, u32[]{:S(2)}, u32[]{:S(2)}) collective-permute-start(bf16[1,64,2048]{2,1,0:T(8,128)(2,1)S(1)} %get-tuple-element.24), channel_id=1, source_target_pairs={{1,0},{2,1},{3,2},{4,3},{5,4},{6,5},{7,6},{8,7},{9,8},{10,9},{11,1... | collective-permute-start | bytes 786440 | tf_op jit(solution)/shard_map/ppermute | solution.py:20
  96.7 5.2 %collective-permute-start.22 = (bf16[1,64,2048]{2,1,0:T(8,128)(2,1)S(1)}, bf16[1,64,2048]{2,1,0:T(8,128)(2,1)S(1)}, u32[]{:S(2)}, u32[]{:S(2)}) collective-permute-start(bf16[1,64,2048]{2,1,0:T(8,128)(2,1)S(1)} %get-tuple-element.23), channel_id=1, source_target_pairs={{0,1},{1,2},{2,3},{3,4},{4,5},{5,6},{6,7},{7,8},{8,9},{9,10},{10,1... | collective-permute-start | bytes 786440 | tf_op jit(solution)/shard_map/ppermute | solution.py:17
  99.1 4.6 %collective-permute-start.15 = (f32[20,641]{1,0:T(8,128)S(1)}, f32[20,641]{1,0:T(8,128)S(1)}, u32[]{:S(2)}, u32[]{:S(2)}) collective-permute-start(f32[20,641]{1,0:T(8,128)S(1)} %pad_maximum_fusion.5), channel_id=1, source_target_pairs={{0,24},{1,25},{2,26},{3,27},{4,28},{5,29},{6,30},{7,31},{8,0},{9,1... | collective-permute-start | bytes 153848 | tf_op jit(solution)/shard_map/ppermute | solution.py:53
  99.6 8.2 %collective-permute-start.16 = (f32[20,641]{1,0:T(8,128)S(1)}, f32[20,641]{1,0:T(8,128)S(1)}, u32[]{:S(2)}, u32[]{:S(2)}) collective-permute-start(f32[20,641]{1,0:T(8,128)S(1)} %pad_maximum_fusion.5), channel_id=1, source_target_pairs={{0,16},{1,17},{2,18},{3,19},{4,20},{5,21},{6,22},{7,23},{8,24},{9,... | collective-permute-start | bytes 153848 | tf_op jit(solution)/shard_map/ppermute | solution.py:53
  100.1 7.8 %collective-permute-start.17 = (f32[20,641]{1,0:T(8,128)S(1)}, f32[20,641]{1,0:T(8,128)S(1)}, u32[]{:S(2)}, u32[]{:S(2)}) collective-permute-start(f32[20,641]{1,0:T(8,128)S(1)} %pad_maximum_fusion.5), channel_id=1, source_target_pairs={{0,8},{1,9},{2,10},{3,11},{4,12},{5,13},{6,14},{7,15},{8,16},{9,17... | collective-permute-start | bytes 153848 | tf_op jit(solution)/shard_map/ppermute | solution.py:53
  108.0 7.0 %collective-permute-start.18 = (f32[80,641]{1,0:T(8,128)S(1)}, f32[80,641]{1,0:T(8,128)S(1)}, u32[]{:S(2)}, u32[]{:S(2)}) collective-permute-start(f32[80,641]{1,0:T(8,128)S(1)} %pad_maximum_fusion.4), channel_id=1, source_target_pairs={{0,6},{1,7},{2,0},{3,1},{4,2},{5,3},{6,4},{7,5},{8,14},{9,15},{10,... | collective-permute-start | bytes 615368 | tf_op jit(solution)/shard_map/ppermute | solution.py:53
  108.3 8.6 %collective-permute-start.19 = (f32[80,641]{1,0:T(8,128)S(1)}, f32[80,641]{1,0:T(8,128)S(1)}, u32[]{:S(2)}, u32[]{:S(2)}) collective-permute-start(f32[80,641]{1,0:T(8,128)S(1)} %pad_maximum_fusion.4), channel_id=1, source_target_pairs={{0,4},{1,5},{2,6},{3,7},{4,0},{5,1},{6,2},{7,3},{8,12},{9,13},{10,... | collective-permute-start | bytes 615368 | tf_op jit(solution)/shard_map/ppermute | solution.py:53
  108.5 14.5 %collective-permute-start.20 = (f32[80,641]{1,0:T(8,128)S(1)}, f32[80,641]{1,0:T(8,128)S(1)}, u32[]{:S(2)}, u32[]{:S(2)}) collective-permute-start(f32[80,641]{1,0:T(8,128)S(1)} %pad_maximum_fusion.4), channel_id=1, source_target_pairs={{0,2},{1,3},{2,4},{3,5},{4,6},{5,7},{6,0},{7,1},{8,10},{9,11},{10,... | collective-permute-start | bytes 615368 | tf_op jit(solution)/shard_map/ppermute | solution.py:53
  123.2 4.6 %collective-permute-start.21 = (f32[320,641]{1,0:T(8,128)S(1)}, f32[320,641]{1,0:T(8,128)S(1)}, u32[]{:S(2)}, u32[]{:S(2)}) collective-permute-start(f32[320,641]{1,0:T(8,128)S(1)} %pad_maximum_fusion.2), channel_id=1, source_target_pairs={{0,1},{1,0},{2,3},{3,2},{4,5},{5,4},{6,7},{7,6},{8,9},{9,8},{10,11... | collective-permute-start | bytes 2461448 | tf_op jit(solution)/shard_map/ppermute | solution.py:53
  130.8 6.3 %copy-start.5 = (f32[576,576]{1,0:T(8,128)S(1)}, f32[576,576]{1,0:T(8,128)}, u32[]{:S(2)}) copy-start(f32[576,576]{1,0:T(8,128)} %get-tuple-element.16) | copy-start | bytes 3981316
  178.2 14.9 %slice-start = ((s8[7864320]{0:T(1024)(128)(4,1)}), s8[4194304]{0:T(1024)(128)(4,1)S(1)}, s32[]{:S(2)}) async-start(s8[7864320]{0:T(1024)(128)(4,1)} %bitcast.144), calls=%async_computation | async-start | bytes 8388608
  184.4 8.7 %slice-start.1 = ((s8[7864320]{0:T(1024)(128)(4,1)}), s8[3670016]{0:T(1024)(128)(4,1)S(1)}, s32[]{:S(2)}) async-start(s8[7864320]{0:T(1024)(128)(4,1)} %bitcast.144), calls=%async_computation.1 | async-start | bytes 7340032
  196.5 3.5 %copy-start.6 = (f32[64]{0:T(128)S(1)}, f32[64]{0:T(128)}, u32[]{:S(2)}) copy-start(f32[64]{0:T(128)} %param.6) | copy-start | bytes 772
  228.6 2.5 %copy-start.4 = (f32[576,576]{1,0:T(8,128)S(1)}, f32[576,576]{1,0:T(8,128)}, u32[]{:S(2)}) copy-start(f32[576,576]{1,0:T(8,128)} %copy-done.3) | copy-start | bytes 3981316
  (1 other events, 1.2 us)
